TPU v7x, 32 devices: a whole 2x2x4 slice. The times are simulated.
32 devices in a mesh: row: 4 (over z), col: 4 (over y, core), pix: 2 (over x).
Axes of the slice: x: 2, y: 2, z: 4, core: 2. Of those that a mesh axis runs over, the one named last changes fastest.
Arguments:
- sample_frames: bfloat16 [4096, 16384], P(('row', 'col'), 'pix'), may hold values from 0.14 to 26
- reference_frames: bfloat16 [4096, 16384], P(('row', 'col'), 'pix'), may hold values from 0.14 to 26
- gain: float32 [16384], P('pix'), may hold values from 0.5 to 2
- flat: float32 [16384], P('pix'), may hold values from 0.6 to 1.6
- qbin: int32 [16384], P('pix'), may hold values from 0 to 31
- region: int32 [16384], P('pix'), may hold values 0 or 1
- live: int32 [16384], P('pix'), may hold values 0 or 1
Outputs:
- twotime: float32 [4096, 4, 4, 256], P('row', None, 'col', 'pix')
All inputs are finite; a program needn't handle non-finite values. No bound on the sum of `region` or of `live` on one device may be relied on, other than what follows from the above.
Results may differ from a plain program's by a relative error of at most 0.0039.
Values may be sent and summed in bfloat16 or wider, within the bound.
No kernel may reach another device: no remote copies, remote signals or barrier semaphores. Data moves between devices by JAX's collectives and lax.ppermute only.
A program may use at most 128 MiB of HBM per device.

v0:
```python
import math
import jax
import jax.numpy as jnp
from jax import lax
from jax.sharding import PartitionSpec as P

QBINS = 32


def on_device(sample_frames, reference_frames, gain, flat, qbin, region, live):
    block = sample_frames.shape[0]
    factor = gain / flat
    select = (qbin[None, :] == jnp.arange(QBINS, dtype=jnp.int32)[:, None]).astype(jnp.float32)
    ref_select = select * (live * (1 - region)).astype(jnp.float32)[None, :]
    sample_weight = (live * region).astype(jnp.float32)
    corrected_sample = sample_frames.astype(jnp.float32) * factor
    corrected_reference = reference_frames.astype(jnp.float32) * factor
    sums_sample = jnp.dot(corrected_sample, ref_select.T, precision=lax.Precision.HIGHEST)
    sums_reference = jnp.dot(corrected_reference, ref_select.T, precision=lax.Precision.HIGHEST)
    counts = jnp.sum(ref_select, axis=1)
    sums_sample, sums_reference, counts = lax.psum((sums_sample, sums_reference, counts), "pix")
    mean_sample = (sums_sample + 1.0) / (counts + 1.0)
    mean_reference = (sums_reference + 1.0) / (counts + 1.0)
    spread_sample = jnp.dot(mean_sample, select, precision=lax.Precision.HIGHEST)
    spread_reference = jnp.dot(mean_reference, select, precision=lax.Precision.HIGHEST)
    delta_sample = ((corrected_sample / spread_sample - 1.0) * sample_weight).astype(jnp.bfloat16)
    delta_reference = (corrected_reference / spread_reference - 1.0).astype(jnp.bfloat16)
    sample_rows = lax.all_gather(delta_sample, "col", axis=0, tiled=True)
    partial_value = lax.dot_general(
        sample_rows,
        lax.all_gather(delta_reference, "row", axis=0, tiled=True),
        (((1,), (1,)), ((), ())),
        preferred_element_type=jnp.float32,
    )
    groups = lax.axis_size("row")
    scale = 1.0 / math.sqrt(gain.shape[0] * lax.axis_size("pix"))
    partial_value = (partial_value * scale).reshape(sample_rows.shape[0], groups, block)
    whole = lax.psum(partial_value, "pix")
    width = block // lax.axis_size("pix")
    mine = lax.dynamic_slice_in_dim(whole, lax.axis_index("pix") * width, width, 2)
    return mine[:, :, None, :]


def solution(mesh):
    return jax.shard_map(
        on_device,
        mesh=mesh,
        in_specs=(
            P(("row", "col"), "pix"),
            P(("row", "col"), "pix"),
            P("pix"),
            P("pix"),
            P("pix"),
            P("pix"),
            P("pix"),
        ),
        out_specs=P("row", None, "col", "pix"),
        check_vma=False,
    )
```

profile of v0, /device:TPU:0, one launch (start us, length us, event | category | flops | bytes accessed | tf_op | source)
XLA Modules:
  0.0 598.4 jit_solution(18286605986021742596)
XLA Ops:
  6.5 0.0 copy-start
  6.5 0.0 all-reduce.6.cloned.1.call-start
  6.5 0.8 multiply_convert_fusion.1
  7.3 0.8 div.23
  8.1 1.5 select_reduce_fusion
  9.6 9.2 %fusion.5 = f32[256,32]{1,0:T(8,128)} fusion(bf16[256,8192]{1,0:T(8,128)(2,1)} %param.8, f32[8192]{0:T(1024)S(1)} %div.23, f32[8192]{0:T(1024)S(1)} %get-tuple-element.8, s32[8192]{0:T(1024)} %param.11), kind=kOutput, calls=%fused_computation.8 | convolution fusion | flops 810024960 | bytes 4325376 | tf_op jit(solution)/shard_map/dot_general | solution.py:19
  18.8 9.2 %fusion.6 = f32[256,32]{1,0:T(8,128)} fusion(bf16[256,8192]{1,0:T(8,128)(2,1)} %param.7, f32[8192]{0:T(1024)S(1)} %div.23, f32[8192]{0:T(1024)S(1)} %get-tuple-element.8, s32[8192]{0:T(1024)} %param.11), kind=kOutput, calls=%fused_computation.10 | convolution fusion | flops 810024960 | bytes 4325376 | tf_op jit(solution)/shard_map/dot_general | solution.py:18
  28.0 0.0 all-reduce.6.cloned.1.call-update
  28.1 0.0 all-gather.3.cloned.1.call-start
  28.1 26.4 %all-reduce.6.cloned.1.call-done = (f32[256,32]{1,0:T(8,128)}, f32[32]{0:T(128)}, f32[256,32]{1,0:T(8,128)}) async-done(((f32[256,32]{1,0:T(8,128)}, f32[32]{0:T(128)}, f32[256,32]{1,0:T(8,128)}), (f32[256,32]{1,0:T(8,128)}, f32[32]{0:T(128)}, f32[256,32]{1,0:T(8,128)})) %all-reduce.6.cloned.1.call-update) | async-done | bytes 65680 | tf_op jit(solution)/shard_map/psum | solution.py:21
  54.5 0.6 broadcast_add_fusion
  55.1 0.0 copy-done
  55.1 0.0 copy-start.1
  55.1 7.9 %fusion.4 = bf16[256,8192]{1,0:T(8,128)(2,1)} fusion(bf16[256,8192]{1,0:T(8,128)(2,1)} %param.7, f32[8192]{0:T(1024)S(1)} %get-tuple-element.9, f32[8192]{0:T(1024)S(1)} %div.23, s32[8192]{0:T(1024)S(1)} %copy-done, f32[256,32]{1,0:T(8,128)} %get-tuple-element.5, f32[32]{0:T(128)S(1)} %broadcast_add_fusion), kind=kOutput, calls=%fused_computation.6 | convolution fusion | flops 818167808 | bytes 8519808 | tf_op jit(solution)/shard_map/dot_general | solution.py:24
  63.0 0.0 all-gather.3.cloned.1.call-update
  63.0 0.2 all-gather.5.cloned.1.call-start
  63.3 0.0 copy-done.1
  63.3 7.6 %fusion.1 = bf16[256,8192]{1,0:T(8,128)(2,1)} fusion(bf16[256,8192]{1,0:T(8,128)(2,1)} %param.8, f32[8192]{0:T(1024)S(1)} %div.23, s32[8192]{0:T(1024)S(1)} %copy-done, f32[256,32]{1,0:T(8,128)S(1)} %copy-done.1, f32[32]{0:T(128)S(1)} %broadcast_add_fusion), kind=kOutput, calls=%fused_computation.2 | convolution fusion | flops 816070656 | bytes 8487040 | tf_op jit(solution)/shard_map/dot_general | solution.py:25
  70.9 0.0 all-gather.5.cloned.1.call-update
  70.9 0.0 all-reduce.4.cloned.1.call-start
  70.9 98.4 %all-gather.3.cloned.1.call-done = bf16[1024,8192]{1,0:T(8,128)(2,1)} async-done(((bf16[256,8192]{1,0:T(8,128)(2,1)}), bf16[1024,8192]{1,0:T(8,128)(2,1)}) %all-gather.3.cloned.1.call-update) | async-done | bytes 16777232 | tf_op jit(solution)/shard_map/all_gather | solution.py:28
  169.3 288.5 %all-gather.5.cloned.1.call-done = bf16[1024,8192]{1,0:T(8,128)(2,1)} async-done(((bf16[256,8192]{1,0:T(8,128)(2,1)}), bf16[1024,8192]{1,0:T(8,128)(2,1)}) %all-gather.5.cloned.1.call-update) | async-done | bytes 16777232 | tf_op jit(solution)/shard_map/all_gather | solution.py:31
  457.8 24.3 %convolution_multiply_fusion = f32[1024,1024]{0,1:T(8,128)} fusion(bf16[1024,8192]{1,0:T(8,128)(2,1)} %all-gather.3.cloned.1.call-done, bf16[1024,8192]{1,0:T(8,128)(2,1)} %all-gather.5.cloned.1.call-done), kind=kOutput, calls=%fused_computation.13 | convolution fusion | flops 17180917760 | bytes 37748736 | tf_op jit(solution)/shard_map/dot_general | solution.py:29
  482.1 0.0 all-reduce.4.cloned.1.call-update
  482.1 106.2 %all-reduce.4.cloned.1.call-done = f32[1024,4,256]{0,2,1:T(8,128)} async-done(((f32[1024,4,256]{0,2,1:T(8,128)}), f32[1024,4,256]{0,2,1:T(8,128)}) %all-reduce.4.cloned.1.call-update) | async-done | bytes 4194320 | tf_op jit(solution)/shard_map/psum | solution.py:38
  588.3 1.7 constant_dynamic-slice_fusion
  590.1 1.8 copy.9
Async XLA Ops:
  6.5 48.6 %copy-start = (s32[8192]{0:T(1024)S(1)}, s32[8192]{0:T(1024)}, u32[]{:S(2)}) copy-start(s32[8192]{0:T(1024)} %param.11) | copy-start | bytes 98308
  6.5 48.0 %all-reduce.6.cloned.1.call-start = ((), (), s32[]{:S(2)}) async-start(), calls=%async_computation.3 | async-start | bytes 525312 | tf_op jit(solution)/shard_map/psum | solution.py:21
  28.1 141.3 %all-gather.3.cloned.1.call-start = ((), (), s32[]{:S(2)}) async-start(), calls=%async_computation | async-start | bytes 20971520 | tf_op jit(solution)/shard_map/all_gather | solution.py:28
  55.1 8.2 %copy-start.1 = (f32[256,32]{1,0:T(8,128)S(1)}, f32[256,32]{1,0:T(8,128)}, u32[]{:S(2)}) copy-start(f32[256,32]{1,0:T(8,128)} %get-tuple-element.7) | copy-start | bytes 98308
  63.0 394.8 %all-gather.5.cloned.1.call-start = ((), (), s32[]{:S(2)}) async-start(), calls=%async_computation.1 | async-start | bytes 20971520 | tf_op jit(solution)/shard_map/all_gather | solution.py:31
  70.9 517.4 %all-reduce.4.cloned.1.call-start = ((), (), s32[]{:S(2)}) async-start(), calls=%async_computation.2 | async-start | bytes 8388608 | tf_op jit(solution)/shard_map/psum | solution.py:38
Sparse Core Ops, SparseCore 0:
  28.2 26.2 all-reduce.5
  63.2 106.1 all-gather.2
  171.0 286.7 all-gather.4
  482.3 106.0 all-reduce.3
where the time goes:
time: 599 us; the launch traced here: 598 us
  waiting for transfers between devices  519 us (87%)
  matrix products  58.3 us (10%)
  between operations  13.2 us (2%)
    all_gather x1, waiting for transfers between devices, on_device(): lax.all_gather(delta_reference, 'row', axis=0, tiled=True)  288 us
    psum x1, waiting for transfers between devices, on_device(): whole = lax.psum(partial_value, 'pix')  106 us
    all_gather x1, waiting for transfers between devices, on_device(): sample_rows = lax.all_gather(delta_sample, 'col', axis=0, tiled=True)  98.4 us
    psum x1, waiting for transfers between devices, on_device(): lax.psum((sums_sample, sums_reference, counts), 'pix')  26.4 us
    dot_general x1, matrix products, on_device(): lax.dot_general(sample_rows, lax.all_gather(delta_reference, 'row', axis=...  24.3 us
  transfers between devices with their start and end apart: 4, of which 4 were waited for; matrix products, arithmetic and copies ran while one was open for 1% of the time, Pallas kernels for 0%

commit v1 on v0

--- a/solution.py
+++ b/solution.py
@@ -5,6 +5,27 @@
 from jax.sharding import PartitionSpec as P
 
 QBINS = 32
+
+
+def groups_divide(here_x, dimension_no):
+    prior = list(here_x.shape[1:])
+    prior[dimension_no] *= here_x.shape[0]
+    return jnp.moveaxis(here_x, 0, dimension_no).reshape(prior)
+
+
+def reach_domain_in(array_in, across, row_dim):
+    wide_n = lax.psum(1, across)
+    front = range(wide_n)
+    row_out = map(lambda dev_j: (dev_j, (dev_j + 1) % wide_n), front)
+    store = list(row_out)
+    rows = [array_in]
+    while len(rows) < wide_n:
+        built = lax.ppermute(rows[-1], across, store)
+        rows.append(built)
+    found_now = lax.axis_index(across)
+    b_now = jnp.stack(rows, axis=0)
+    rows = b_now[(found_now - jnp.arange(wide_n)) % wide_n]
+    return groups_divide(rows, row_dim)
 
 
 def on_device(sample_frames, reference_frames, gain, flat, qbin, region, live):
@@ -28,7 +49,7 @@
     sample_rows = lax.all_gather(delta_sample, "col", axis=0, tiled=True)
     partial_value = lax.dot_general(
         sample_rows,
-        lax.all_gather(delta_reference, "row", axis=0, tiled=True),
+        reach_domain_in(delta_reference, across="row", row_dim=0),
         (((1,), (1,)), ((), ())),
         preferred_element_type=jnp.float32,
     )

time: 599 us -> 552 us (0.922)
  waiting for transfers between devices: 519 us -> 409 us
  other arithmetic: 3.66 us -> 37.4 us
  local copies, waits for them, and re-layouts: 3.55 us -> 34.5 us
    all_gather x1 -> x0, waiting for transfers between devices: 288 us -> none  [on_device(): lax.all_gather(delta_reference, 'row', axis=0, tiled=True)]
    ppermute x0 -> x3, waiting for transfers between devices: none -> 278 us  [reach_domain_in(): built = lax.ppermute(rows[-1], across, store)]
    all_gather x1, waiting for transfers between devices: 98.4 us -> 0.01 us  [on_device(): sample_rows = lax.all_gather(delta_sample, 'col', axis=0, tiled=True)]
    gather x0 -> x4, local copies, waits for them, and re-layouts: none -> 26.9 us  [reach_domain_in(): rows = b_now[(found_now - jnp.arange(wide_n)) % wide_n]]
    another operation x0 -> x1, other arithmetic: none -> 13.9 us  [reach_domain_in(): b_now = jnp.stack(rows, axis=0)]
    unnamed x0 -> x1, other arithmetic: none -> 13.7 us
  transfers between devices with their start and end apart: 4 -> 6, of which waited for: 4 -> 5; matrix products, arithmetic and copies ran while one was open for 1% -> 12% of each run, Pallas kernels for 0% -> 0%
where the time goes in v1:
time: 552 us
  waiting for transfers between devices  409 us (74%)
  matrix products  55.1 us (10%)
  other arithmetic  37.4 us (7%)
  local copies, waits for them, and re-layouts  34.5 us (6%)
  between operations  13.2 us (2%)
    ppermute x3, waiting for transfers between devices, reach_domain_in(): built = lax.ppermute(rows[-1], across, store)  278 us
    psum x1, waiting for transfers between devices, on_device(): whole = lax.psum(partial_value, 'pix')  105 us
    gather x4, local copies, waits for them, and re-layouts, reach_domain_in(): rows = b_now[(found_now - jnp.arange(wide_n)) % wide_n]  26.9 us
    psum x1, waiting for transfers between devices, on_device(): lax.psum((sums_sample, sums_reference, counts), 'pix')  26.2 us
    dot_general x1, matrix products, on_device(): lax.dot_general(sample_rows, reach_domain_in(delta_reference, across='row...  24.3 us
    another operation x1, other arithmetic, reach_domain_in(): b_now = jnp.stack(rows, axis=0)  13.9 us
    unnamed x1, other arithmetic  13.7 us
  transfers between devices with their start and end apart: 6, of which 5 were waited for; matrix products, arithmetic and copies ran while one was open for 12% of the time, Pallas kernels for 0%

profile of v1, /device:TPU:0, one launch (start us, length us, event | category | flops | bytes accessed | tf_op | source)
XLA Modules:
  0.0 551.5 jit_solution(4250039349875588054)
XLA Ops:
  6.5 0.9 multiply_convert_fusion.1
  7.5 1.1 div.23
  8.6 1.5 select_reduce_fusion
  10.1 9.2 %fusion.5 = f32[256,32]{1,0:T(8,128)} fusion(bf16[256,8192]{1,0:T(8,128)(2,1)} %param.8, f32[8192]{0:T(1024)S(1)} %div.23, f32[8192]{0:T(1024)S(1)} %get-tuple-element.10, s32[8192]{0:T(1024)} %param.11), kind=kOutput, calls=%fused_computation.13 | convolution fusion | flops 810024960 | bytes 4325376 | tf_op jit(solution)/shard_map/dot_general | solution.py:40
  19.4 7.3 %fusion.6 = f32[256,32]{1,0:T(8,128)} fusion(bf16[256,8192]{1,0:T(8,128)(2,1)S(1)} %copy-done.3, f32[8192]{0:T(1024)S(1)} %div.23, f32[8192]{0:T(1024)S(1)} %get-tuple-element.10, s32[8192]{0:T(1024)S(1)} %copy-done.2), kind=kOutput, calls=%fused_computation.15 | convolution fusion | flops 810024960 | bytes 4325376 | tf_op jit(solution)/shard_map/dot_general | solution.py:39
  26.7 0.0 all-reduce.6.cloned.1.call-update
  26.7 0.2 all-gather.2.cloned.1.call-start
  26.9 26.2 %all-reduce.6.cloned.1.call-done = (f32[256,32]{1,0:T(8,128)}, f32[32]{0:T(128)}, f32[256,32]{1,0:T(8,128)}) async-done(((f32[256,32]{1,0:T(8,128)}, f32[32]{0:T(128)}, f32[256,32]{1,0:T(8,128)}), (f32[256,32]{1,0:T(8,128)}, f32[32]{0:T(128)}, f32[256,32]{1,0:T(8,128)})) %all-reduce.6.cloned.1.call-update) | async-done | bytes 65680 | tf_op jit(solution)/shard_map/psum | solution.py:42
  53.1 0.7 broadcast_add_fusion
  53.8 8.1 %fusion.4 = bf16[256,8192]{1,0:T(8,128)(2,1)} fusion(bf16[256,8192]{1,0:T(8,128)(2,1)} %param.7, f32[8192]{0:T(1024)S(1)} %get-tuple-element.11, f32[8192]{0:T(1024)S(1)} %div.23, s32[8192]{0:T(1024)S(1)} %copy-done.2, f32[256,32]{1,0:T(8,128)} %get-tuple-element.5, f32[32]{0:T(128)S(1)} %broadcast_add_fusion), kind=kOutput, calls=%fused_computation.11 | convolution fusion | flops 818167808 | bytes 8519808 | tf_op jit(solution)/shard_map/dot_general | solution.py:45
  61.9 0.0 all-gather.2.cloned.1.call-update
  61.9 0.0 all-reduce.4.cloned.1.call-start
  61.9 6.2 %fusion.1 = bf16[256,8192]{1,0:T(8,128)(2,1)S(1)} fusion(bf16[256,8192]{1,0:T(8,128)(2,1)} %param.8, f32[8192]{0:T(1024)S(1)} %div.23, s32[8192]{0:T(1024)S(1)} %copy-done.2, f32[256,32]{1,0:T(8,128)S(1)} %copy-done.4, f32[32]{0:T(128)S(1)} %broadcast_add_fusion), kind=kOutput, calls=%fused_computation.7 | convolution fusion | flops 816070656 | bytes 8487040 | tf_op jit(solution)/shard_map/dot_general | solution.py:46
  68.2 2.1 copy-done
  70.3 1.5 collective-permute-start
  71.8 92.5 %collective-permute-done = bf16[256,8192]{1,0:T(8,128)(2,1)S(1)} collective-permute-done((bf16[256,8192]{1,0:T(8,128)(2,1)S(1)}, bf16[256,8192]{1,0:T(8,128)(2,1)S(1)}, u32[]{:S(2)}, u32[]{:S(2)}) %collective-permute-start) | collective-permute-done | bytes 4194336 | tf_op jit(solution)/shard_map/ppermute | solution.py:23
  164.3 2.0 copy-done.1
  166.2 0.0 collective-permute-start.1
  166.2 93.1 %collective-permute-done.1 = bf16[256,8192]{1,0:T(8,128)(2,1)} collective-permute-done((bf16[256,8192]{1,0:T(8,128)(2,1)S(1)}, bf16[256,8192]{1,0:T(8,128)(2,1)}, u32[]{:S(2)}, u32[]{:S(2)}) %collective-permute-start.1) | collective-permute-done | bytes 4194336 | tf_op jit(solution)/shard_map/ppermute | solution.py:23
  259.4 92.4 %collective-permute-done.2 = bf16[256,8192]{1,0:T(8,128)(2,1)} collective-permute-done((bf16[256,8192]{1,0:T(8,128)(2,1)}, bf16[256,8192]{1,0:T(8,128)(2,1)}, u32[]{:S(2)}, u32[]{:S(2)}) %collective-permute-start.2) | collective-permute-done | bytes 4194336 | tf_op jit(solution)/shard_map/ppermute | solution.py:23
  351.8 13.9 %pad_maximum_fusion = bf16[4,256,8192]{2,1,0:T(8,128)(2,1)} fusion(bf16[1,256,8192]{2,1,0:T(8,128)(2,1)} %bitcast.3, bf16[1,256,8192]{2,1,0:T(8,128)(2,1)} %bitcast.2, bf16[1,256,8192]{2,1,0:T(8,128)(2,1)} %bitcast.14, bf16[1,256,8192]{2,1,0:T(8,128)(2,1)} %bitcast.12), kind=kLoop, calls=%fused_computation.3 | loop fusion | flops 25165824 | bytes 33554432 | tf_op jit(solution)/shard_map/stack | solution.py:26
  365.7 9.3 %fusion.33 = (bf16[4,256,2816]{2,1,0:T(8,128)(2,1)}, bf16[4,256,2816]{2,1,0:T(8,128)(2,1)}) fusion(bf16[4,256,8192]{2,1,0:T(8,128)(2,1)} %pad_maximum_fusion), kind=kLoop, calls=%fused_computation.55 | loop fusion | bytes 23068672 | tf_op jit(solution)/shard_map/gather | solution.py:27
  374.9 6.0 %gather_fusion = bf16[4,256,2816]{2,1,0:T(8,128)(2,1)} fusion(bf16[4,256,2816]{2,1,0:T(8,128)(2,1)} %get-tuple-element.8, s32[1024]{0:T(1024)S(1)} %pad_clamp_fusion), kind=kCustom, calls=%fused_computation | custom fusion | bytes 11534352 | tf_op jit(solution)/shard_map/gather | solution.py:27
  380.9 6.0 %gather_fusion.1 = bf16[4,256,2816]{2,1,0:T(8,128)(2,1)} fusion(bf16[4,256,2816]{2,1,0:T(8,128)(2,1)} %get-tuple-element.9, s32[1024]{0:T(1024)S(1)} %pad_clamp_fusion), kind=kCustom, calls=%fused_computation.1 | custom fusion | bytes 11534352 | tf_op jit(solution)/shard_map/gather | solution.py:27
  386.9 5.6 %pad_maximum_fusion.2 = bf16[4,256,2560]{2,1,0:T(8,128)(2,1)} fusion(bf16[1,256,8192]{2,1,0:T(8,128)(2,1)} %bitcast.3, bf16[1,256,8192]{2,1,0:T(8,128)(2,1)} %bitcast.2, bf16[1,256,8192]{2,1,0:T(8,128)(2,1)} %bitcast.15, bf16[1,256,8192]{2,1,0:T(8,128)(2,1)} %bitcast.13), kind=kLoop, calls=%fused_computation.16 | loop fusion | flops 20971520 | bytes 22020096 | tf_op jit(solution)/shard_map/gather | solution.py:27
  392.5 5.6 %gather_fusion.2 = bf16[4,256,2560]{2,1,0:T(8,128)(2,1)} fusion(bf16[4,256,2560]{2,1,0:T(8,128)(2,1)} %pad_maximum_fusion.2, s32[1024]{0:T(1024)S(1)} %pad_clamp_fusion), kind=kCustom, calls=%fused_computation.2 | custom fusion | bytes 10485776 | tf_op jit(solution)/shard_map/gather | solution.py:27
  398.1 13.7 %pad_maximum_fusion.1 = bf16[4,256,8192]{2,1,0:T(8,128)(2,1)} fusion(bf16[4,256,2560]{2,1,0:T(8,128)(2,1)} %gather_fusion.2, bf16[4,256,2816]{2,1,0:T(8,128)(2,1)} %gather_fusion.1, bf16[4,256,2816]{2,1,0:T(8,128)(2,1)} %gather_fusion), kind=kLoop, calls=%fused_computation.4 | loop fusion | flops 50331648 | bytes 33554432
  411.8 24.3 %convolution_multiply_fusion = f32[1024,1024]{0,1:T(8,128)} fusion(bf16[1024,8192]{1,0:T(8,128)(2,1)} %all-gather.2.cloned.1.call-done, bf16[1024,8192]{1,0:T(8,128)(2,1)} %bitcast.11), kind=kOutput, calls=%fused_computation.19 | convolution fusion | flops 17180917760 | bytes 37748736 | tf_op jit(solution)/shard_map/dot_general | solution.py:50
  436.1 0.0 all-reduce.4.cloned.1.call-update
  436.2 105.3 %all-reduce.4.cloned.1.call-done = f32[1024,4,256]{0,2,1:T(8,128)} async-done(((f32[1024,4,256]{0,2,1:T(8,128)}), f32[1024,4,256]{0,2,1:T(8,128)}) %all-reduce.4.cloned.1.call-update) | async-done | bytes 4194320 | tf_op jit(solution)/shard_map/psum | solution.py:59
  541.4 1.7 constant_dynamic-slice_fusion
  543.2 1.8 copy.9
  (13 shorter events, 0.0 us)
Async XLA Ops:
  6.5 12.8 %copy-start.2 = (s32[8192]{0:T(1024)S(1)}, s32[8192]{0:T(1024)}, u32[]{:S(2)}) copy-start(s32[8192]{0:T(1024)} %param.11) | copy-start | bytes 98308
  6.5 46.6 %all-reduce.6.cloned.1.call-start = ((), (), s32[]{:S(2)}) async-start(), calls=%async_computation.2 | async-start | bytes 525312 | tf_op jit(solution)/shard_map/psum | solution.py:42
  6.5 12.8 %copy-start.3 = (bf16[256,8192]{1,0:T(8,128)(2,1)S(1)}, bf16[256,8192]{1,0:T(8,128)(2,1)}, u32[]{:S(2)}) copy-start(bf16[256,8192]{1,0:T(8,128)(2,1)} %param.7) | copy-start | bytes 12582916
  26.7 385.1 %all-gather.2.cloned.1.call-start = ((), (), s32[]{:S(2)}) async-start(), calls=%async_computation | async-start | bytes 20971520 | tf_op jit(solution)/shard_map/all_gather | solution.py:49
  53.8 8.1 %copy-start.4 = (f32[256,32]{1,0:T(8,128)S(1)}, f32[256,32]{1,0:T(8,128)}, u32[]{:S(2)}) copy-start(f32[256,32]{1,0:T(8,128)} %get-tuple-element.7) | copy-start | bytes 98308
  61.9 479.6 %all-reduce.4.cloned.1.call-start = ((), (), s32[]{:S(2)}) async-start(), calls=%async_computation.1 | async-start | bytes 8388608 | tf_op jit(solution)/shard_map/psum | solution.py:59
  68.2 2.1 copy-start
  70.3 93.9 %collective-permute-start = (bf16[256,8192]{1,0:T(8,128)(2,1)S(1)}, bf16[256,8192]{1,0:T(8,128)(2,1)S(1)}, u32[]{:S(2)}, u32[]{:S(2)}) collective-permute-start(bf16[256,8192]{1,0:T(8,128)(2,1)S(1)} %fusion.1), channel_id=1, source_target_pairs={{0,8},{8,16},{16,24},{24,0},{1,9},{9,17},{17,25},{25,1},{2,10},{10... | collective-permute-start | bytes 12582920 | tf_op jit(solution)/shard_map/ppermute | solution.py:23
  164.3 2.0 copy-start.1
  166.2 93.1 %collective-permute-start.1 = (bf16[256,8192]{1,0:T(8,128)(2,1)S(1)}, bf16[256,8192]{1,0:T(8,128)(2,1)}, u32[]{:S(2)}, u32[]{:S(2)}) collective-permute-start(bf16[256,8192]{1,0:T(8,128)(2,1)S(1)} %collective-permute-done), channel_id=1, source_target_pairs={{0,8},{8,16},{16,24},{24,0},{1,9},{9,17},{17,25},{25,1},{2,10},{10... | collective-permute-start | bytes 12582920 | tf_op jit(solution)/shard_map/ppermute | solution.py:23
  259.4 92.4 %collective-permute-start.2 = (bf16[256,8192]{1,0:T(8,128)(2,1)}, bf16[256,8192]{1,0:T(8,128)(2,1)}, u32[]{:S(2)}, u32[]{:S(2)}) collective-permute-start(bf16[256,8192]{1,0:T(8,128)(2,1)} %collective-permute-done.1), channel_id=1, source_target_pairs={{0,8},{8,16},{16,24},{24,0},{1,9},{9,17},{17,25},{25,1},{2,10},{10... | collective-permute-start | bytes 12582920 | tf_op jit(solution)/shard_map/ppermute | solution.py:23
Sparse Core Ops, SparseCore 0:
  26.8 26.2 all-reduce.5
  62.0 106.1 all-gather.1
  436.3 105.1 all-reduce.3
